TPU v7x, 256 devices: a whole 4x4x8 slice. The times are simulated.
256 devices in a mesh: bus: 16 (over y, z_hi), line: 16 (over z_lo, x, core).
Axes of the slice: x: 4, y: 4, z: 8 (z_hi: 4, z_lo: 2; z = z_hi * 2 + z_lo), core: 2. Of those that a mesh axis runs over, the one named last changes fastest.
Arguments:
- generation: bfloat16 [1024, 16384], P(None, 'bus'), may hold values from -6 to 6
- profiles: float32 [24, 16384], P(None, 'bus'), may hold values from -5 to 5
- scen_profile: int32 [1024], replicated, may hold values from 0 to 23
- ptdf: bfloat16 [16384, 16384], P('line', 'bus'), may hold values from -0.046875 to 0.046875
- lodf: float32 [6144, 512], P('line'), may hold values from -1 to 1
- limits: float32 [6144], P('line'), may hold values from 0.5 to 2
- monitored: int32 [6144], P('line'), may hold values from 0 to 16383, as said below
- outages: int32 [512], replicated, may hold values from 0 to 16383, as said below
- cost_quad: float32 [16384], P('bus'), may hold values from 0.5 to 2
Outputs:
- gradient: bfloat16 [1024, 16384], P('line', 'bus')
- outage_flow: float32 [1024, 512], P('bus')
- outage_sens: float32 [1024, 512], P('bus')
Inputs may be any that keep to these rules, and one draw needn't show every extreme that they name: `monitored`: the entries with positions k * 384 to (k + 1) * 384 - 1 are distinct line ids of the k-th block of 1024 lines (ids k * 1024 to (k + 1) * 1024 - 1). `outages`: distinct line ids; how many fall in each block of 1024 lines varies from block to block.
All inputs are finite; a program needn't handle non-finite values.
Results may differ from a plain program's by a relative error of at most 0.0029.
Values may be sent and summed in bfloat16 or wider, within the bound.
No kernel may reach another device: no remote copies, remote signals or barrier semaphores. Data moves between devices by JAX's collectives and lax.ppermute only.
A program may use at most 64 MiB of HBM per device.

v0:
```python
import math
import jax
import jax.numpy as jnp
from jax import lax
from jax.sharding import PartitionSpec as P

sharpness = 4.0


def contingency(pieces, lodf, limits, outage_total):
    base_block, outage_block = pieces
    post_flow = base_block[:, :, None] + lodf[None, :, :] * outage_block[:, None, :]
    bounds = limits[None, :, None]
    raw_slope = jax.nn.sigmoid(sharpness * (post_flow - bounds)) - jax.nn.sigmoid(
        sharpness * (-post_flow - bounds)
    )
    direct = jnp.sum(raw_slope, axis=2) / outage_total
    sens_part = jnp.einsum("smk,mk->sk", raw_slope, lodf, precision=lax.Precision.HIGHEST)
    return (direct, sens_part)


def on_device(
    generation, profiles, scen_profile, ptdf, lodf, limits, monitored, outages, cost_quad
):
    line_count = lax.axis_size("line")
    profile_count = profiles.shape[0]
    profile_pick = (
        scen_profile[:, None] == jnp.arange(profile_count, dtype=jnp.int32)[None, :]
    ).astype(jnp.float32)
    loads = jnp.dot(profile_pick, profiles, precision=lax.Precision.HIGHEST)
    injection = (generation.astype(jnp.float32) - loads).astype(jnp.bfloat16)
    scen_rows = injection.shape[0] // lax.axis_size("bus")
    line_rows = ptdf.shape[0]
    first_line = lax.axis_index("line") * line_rows
    local_monitored = monitored - first_line
    monitor_count = monitored.shape[0]
    outage_total = outages.shape[0]
    monitored_total = monitor_count * line_count
    rel_outages = outages - first_line
    in_block = (rel_outages >= 0) & (rel_outages < line_rows)
    outage_rows = jnp.where(
        in_block[:, None],
        jnp.take(ptdf, jnp.clip(rel_outages, 0, line_rows - 1), axis=0),
        jnp.zeros((), ptdf.dtype),
    )
    my_outage_rows = lax.psum_scatter(outage_rows, "line", scatter_dimension=0, tiled=True)
    monitored_rows = jnp.take(ptdf, local_monitored, axis=0)
    rows = jnp.concatenate([monitored_rows, my_outage_rows], axis=0)
    flow_part = lax.dot_general(
        injection, rows, (((1,), (1,)), ((), ())), preferred_element_type=jnp.float32
    )
    flow_field = lax.psum_scatter(flow_part, "bus", scatter_dimension=0, tiled=True)
    base = flow_field[:, :monitor_count]
    outflow = lax.all_gather(flow_field[:, monitor_count:], "line", axis=1, tiled=True)
    block_size = math.gcd(scen_rows, 4)
    base_blocks = base.reshape(scen_rows // block_size, block_size, monitor_count)
    outage_blocks = outflow.reshape(scen_rows // block_size, block_size, outage_total)
    direct, sens_part = lax.map(
        lambda pieces: contingency(pieces, lodf, limits, outage_total), (base_blocks, outage_blocks)
    )
    direct = direct.reshape(scen_rows, monitor_count)
    sens_part = sens_part.reshape(scen_rows, outage_total)
    matches = (outages[:, None] == monitored[None, :]).astype(jnp.float32)
    flag_part = jnp.sum(matches, axis=1)
    extended = jnp.concatenate(
        [sens_part, flag_part[None, :], jnp.zeros((7, outage_total), jnp.float32)], axis=0
    )
    mine = lax.psum_scatter(extended, "line", scatter_dimension=1, tiled=True)
    sens_mine = mine[:scen_rows]
    flag_mine = mine[scen_rows]
    sens_total = lax.all_gather(sens_mine, "line", axis=1, tiled=True)
    backward = sens_total / outage_total
    outage_sens = sens_total / math.sqrt(monitored_total)
    adjoint_monitored = (
        direct + jnp.dot(backward, matches, precision=lax.Precision.HIGHEST)
    ).astype(jnp.bfloat16)
    adjoint_outage = jnp.where(flag_mine[None, :] > 0.5, 0.0, sens_mine / outage_total).astype(
        jnp.bfloat16
    )
    piece = jnp.concatenate([adjoint_monitored, adjoint_outage], axis=1)
    all_piece = lax.all_gather(piece, "bus", axis=0, tiled=True)
    grad_rows = all_piece.shape[0] // line_count
    pushed = lax.psum_scatter(
        jnp.dot(all_piece, rows, preferred_element_type=jnp.float32),
        "line",
        scatter_dimension=0,
        tiled=True,
    )
    own_generation = lax.dynamic_slice_in_dim(
        generation, lax.axis_index("line") * grad_rows, grad_rows, 0
    ).astype(jnp.float32)
    gradient = (cost_quad[None, :] * own_generation + pushed).astype(jnp.bfloat16)
    return (gradient, outflow, outage_sens)


def solution(mesh):
    placed = (
        P(None, "bus"),
        P(None, "bus"),
        P(),
        P("line", "bus"),
        P("line", None),
        P("line"),
        P("line"),
        P(),
        P("bus"),
    )
    return jax.shard_map(
        on_device,
        mesh=mesh,
        in_specs=placed,
        out_specs=(P("line", "bus"), P("bus", None), P("bus", None)),
        check_vma=False,
    )
```

profile of v0, /device:TPU:16, one launch (start us, length us, event | category | flops | bytes accessed | tf_op | source)
XLA Modules:
  0.0 532.0 jit_solution(728160581816020870)
XLA Ops:
  15.3 4.9 subtract_convert_fusion
  20.2 59.7 %reduce-scatter.7.cloned.1.call-done = bf16[32,1024]{1,0:T(8,128)(2,1)} async-done(((bf16[512,1024]{1,0:T(8,128)(2,1)}), bf16[32,1024]{1,0:T(8,128)(2,1)}) %reduce-scatter.7.cloned.1.call-update) | async-done | bytes 65552 | tf_op jit(solution)/shard_map/reduce_scatter | solution.py:46
  80.0 4.2 fusion.5
  84.6 86.4 %reduce-scatter.9.cloned.1.call-done = f32[64,416]{1,0:T(8,128)} async-done(((f32[1024,416]{1,0:T(8,128)}), f32[64,416]{1,0:T(8,128)}) %reduce-scatter.9.cloned.1.call-update) | async-done | bytes 106512 | tf_op jit(solution)/shard_map/reduce_scatter | solution.py:52
  172.7 19.4 %all_gather.9 = f32[64,512]{0,1:T(8,128)S(1)} all-gather(f32[64,32]{0,1:T(8,128)S(1)} %copy.22), channel_id=1, replica_groups=mesh['bus'=16,'line'=16] {'line'}, dimensions={1}, use_global_device_ids=true | all-gather | bytes 139264 | tf_op jit(solution)/shard_map/all_gather | solution.py:54
  192.9 128.0 %while.12 = (s32[]{:T(128)}, f32[16,4,384]{2,1,0:T(4,128)}, f32[16,4,512]{2,1,0:T(4,128)}, f32[16,4,384]{2,1,0:T(4,128)S(1)}, f32[384,512]{1,0:T(8,128)}, /*inde...) while((s32[]{:T(128)}, f32[16,4,384]{2,1,0:T(4,128)}, f32[16,4,512]{2,1,0:T(4,128)}, ...), condition=%wide.region_4.5_spmd, body=%wide.region_2.4_spmd.sunk | while | flops 24377344 | bytes 2462829 | solution.py:58
  196.2 3.5 multiply_reduce_fusion.2
  204.2 3.5 multiply_reduce_fusion.2
  212.2 3.5 multiply_reduce_fusion.2
  220.2 3.5 multiply_reduce_fusion.2
  228.2 3.5 multiply_reduce_fusion.2
  236.2 3.5 multiply_reduce_fusion.2
  244.2 3.5 multiply_reduce_fusion.2
  252.2 3.5 multiply_reduce_fusion.2
  260.2 3.5 multiply_reduce_fusion.2
  268.2 3.5 multiply_reduce_fusion.2
  276.2 3.5 multiply_reduce_fusion.2
  284.2 3.5 multiply_reduce_fusion.2
  300.2 3.5 multiply_reduce_fusion.2
  316.2 3.5 multiply_reduce_fusion.2
  323.8 59.1 %reduce-scatter.13.cloned.1.call-done = f32[32,72]{1,0:T(8,128)} async-done(((f32[512,72]{1,0:T(8,128)}), f32[32,72]{1,0:T(8,128)}) %reduce-scatter.13.cloned.1.call-update) | async-done | bytes 9232
  384.5 16.9 %all_gather.10 = f32[64,512]{0,1:T(8,128)S(1)} all-gather(f32[64,32]{0,1:T(8,128)} %bitcast.36), channel_id=1, replica_groups=mesh['bus'=16,'line'=16] {'line'}, dimensions={1}, use_global_device_ids=true | all-gather | bytes 139264 | tf_op jit(solution)/shard_map/all_gather | solution.py:71
  402.1 44.6 %all_gather.11 = bf16[1024,416]{1,0:T(8,128)(2,1)S(1)} all-gather(bf16[64,416]{1,0:T(8,128)(2,1)S(1)} %pad_maximum_fusion.3), channel_id=1, replica_groups=mesh['bus'=16,'line'=16] {'bus'}, dimensions={0}, use_global_device_ids=true | all-gather | bytes 905216 | tf_op jit(solution)/shard_map/all_gather | solution.py:81
  450.7 73.1 %reduce-scatter.11.cloned.1.call-done = f32[64,1024]{1,0:T(8,128)} async-done(((f32[1024,1024]{1,0:T(8,128)}), f32[64,1024]{1,0:T(8,128)}) %reduce-scatter.11.cloned.1.call-update) | async-done | bytes 262160 | tf_op jit(solution)/shard_map/reduce_scatter | solution.py:83
  (143 shorter events, 101.2 us)
Async XLA Ops:
  7.2 1.6 copy-start
  7.2 72.8 %reduce-scatter.7.cloned.1.call-start = ((), (), s32[]{:S(2)}) async-start(), calls=%async_computation.4 | async-start | bytes 1114112 | tf_op jit(solution)/shard_map/reduce_scatter | solution.py:46
  10.8 1.3 copy-start.4
  12.1 158.9 %reduce-scatter.9.cloned.1.call-start = ((), (), s32[]{:S(2)}) async-start(), calls=%async_computation.5 | async-start | bytes 2228224 | tf_op jit(solution)/shard_map/reduce_scatter | solution.py:52
  12.2 3.1 copy-start.3
  12.2 3.1 copy-start.6
  15.3 64.7 %copy-start.1 = (bf16[384,1024]{1,0:T(8,128)(2,1)S(1)}, bf16[384,1024]{1,0:T(8,128)(2,1)}, u32[]{:S(2)}) copy-start(bf16[384,1024]{1,0:T(8,128)(2,1)} %broadcast_select_fusion) | copy-start | bytes 2359300
  20.2 64.1 %copy-start.5 = (s32[512]{0:T(512)S(1)}, s32[512]{0:T(512)}, u32[]{:S(2)}) copy-start(s32[512]{0:T(512)} %param.18) | copy-start | bytes 6148
  84.2 108.1 %copy-start.9 = (f32[384]{0:T(512)S(1)}, f32[384]{0:T(512)}, u32[]{:S(2)}) copy-start(f32[384]{0:T(512)} %param.16) | copy-start | bytes 4612
  84.2 298.7 %reduce-scatter.13.cloned.1.call-start = ((), (), s32[]{:S(2)}) async-start(), calls=%async_computation.7 | async-start | bytes 278528
  192.2 0.7 copy-start.2
  320.9 125.8 %copy-start.8 = (bf16[32,1024]{1,0:T(8,128)(2,1)S(1)}, bf16[32,1024]{1,0:T(8,128)(2,1)}, u32[]{:S(2)}) copy-start(bf16[32,1024]{1,0:T(8,128)(2,1)} %reduce-scatter.7.cloned.1.call-done) | copy-start | bytes 196612
  322.8 201.0 %reduce-scatter.11.cloned.1.call-start = ((), (), s32[]{:S(2)}) async-start(), calls=%async_computation.6 | async-start | bytes 4456448 | tf_op jit(solution)/shard_map/reduce_scatter | solution.py:83
  449.9 73.9 %copy-start.7 = (f32[1024]{0:T(1024)S(1)}, f32[1024]{0:T(1024)}, u32[]{:S(2)}) copy-start(f32[1024]{0:T(1024)} %param.19) | copy-start | bytes 12292
Sparse Core Ops, SparseCore 0:
  12.2 67.7 reduce-scatter.6
  84.3 86.6 reduce-scatter.8
  322.9 59.9 reduce-scatter.12
  450.0 73.7 reduce-scatter.10
where the time goes:
time: 534 us; the launch traced here: 532 us
  waiting for transfers between devices  278 us (52%)
  other arithmetic  124 us (23%)
  blocking collectives  80.9 us (15%)
  local copies, waits for them, and re-layouts  21.5 us (4%)
  between operations  13.9 us (3%)
  matrix products  12.8 us (2%)
    reduce_scatter x1, waiting for transfers between devices, on_device(): lax.psum_scatter(flow_part, 'bus', scatter_dimension=0, tiled=True)  86.4 us
    reduce_scatter x1, waiting for transfers between devices, on_device(): lax.psum_scatter(jnp.dot(all_piece, rows, preferred_element_type=jnp.floa...  73.1 us
    reduce_scatter x1, waiting for transfers between devices, on_device(): lax.psum_scatter(outage_rows, 'line', scatter_dimension=0, tiled=True)  59.7 us
    unnamed x5, waiting for transfers between devices  59.2 us
    dot_general x16, other arithmetic, contingency(): jnp.einsum('smk,mk->sk', raw_slope, lodf, precision=lax.Precision.HIGHEST)  55.3 us
    reduce_sum x16, other arithmetic, contingency(): direct = jnp.sum(raw_slope, axis=2) / outage_total  53.3 us
    all_gather x1, blocking collectives, on_device(): all_piece = lax.all_gather(piece, 'bus', axis=0, tiled=True)  44.6 us
    all_gather x1, blocking collectives, on_device(): lax.all_gather(flow_field[:, monitor_count:], 'line', axis=1, tiled=True)  19.4 us
  transfers between devices with their start and end apart: 4, of which 4 were waited for; matrix products, arithmetic and copies ran while one was open for 2% of the time, Pallas kernels for 0%

commit v1 on v0

--- a/solution.py
+++ b/solution.py
@@ -3,8 +3,14 @@
 import jax.numpy as jnp
 from jax import lax
 from jax.sharding import PartitionSpec as P
+from jax.lax import all_to_all, psum
 
 sharpness = 4.0
+
+
+def drive_patches_up(page, in_dim):
+    outer = jnp.stack(psum(1, "line") * [page], axis=0)
+    return jnp.concatenate(all_to_all(outer, "line", split_axis=0, concat_axis=0), in_dim)
 
 
 def contingency(pieces, lodf, limits, outage_total):
@@ -51,7 +57,7 @@
     )
     flow_field = lax.psum_scatter(flow_part, "bus", scatter_dimension=0, tiled=True)
     base = flow_field[:, :monitor_count]
-    outflow = lax.all_gather(flow_field[:, monitor_count:], "line", axis=1, tiled=True)
+    outflow = drive_patches_up(flow_field[:, monitor_count:], 1)
     block_size = math.gcd(scen_rows, 4)
     base_blocks = base.reshape(scen_rows // block_size, block_size, monitor_count)
     outage_blocks = outflow.reshape(scen_rows // block_size, block_size, outage_total)

time: 534 us -> 516 us (0.966)
  blocking collectives: 80.9 us -> 64.8 us
  local copies, waits for them, and re-layouts: 21.5 us -> 13.1 us
    all_gather x1 -> x0, blocking collectives: 19.4 us -> none  [on_device(): lax.all_gather(flow_field[:, monitor_count:], 'line', axis=1, tiled=True)]
    dynamic_update_slice x16, local copies, waits for them, and re-layouts: 9.57 us -> 0.12 us  [on_device(): lax.map(lambda pieces: contingency(pieces, lodf, limits, outage_total), (...]
    reduce_scatter x1, waiting for transfers between devices: 73.1 us -> 66.7 us  [on_device(): lax.psum_scatter(jnp.dot(all_piece, rows, preferred_element_type=jnp.floa...]
    all_to_all x0 -> x1, waiting for transfers between devices: none -> 5.34 us  [drive_patches_up(): all_to_all(outer, 'line', split_axis=0, concat_axis=0)]
  transfers between devices with their start and end apart: 4 -> 5, of which waited for: 4 -> 5; matrix products, arithmetic and copies ran while one was open for 2% -> 2% of each run, Pallas kernels for 0% -> 0%
where the time goes in v1:
time: 516 us; the launch traced here: 514 us
  waiting for transfers between devices  278 us (54%)
  other arithmetic  126 us (24%)
  blocking collectives  64.8 us (13%)
  between operations  14 us (3%)
  matrix products  13.6 us (3%)
  local copies, waits for them, and re-layouts  13.1 us (3%)
    reduce_scatter x1, waiting for transfers between devices, on_device(): lax.psum_scatter(flow_part, 'bus', scatter_dimension=0, tiled=True)  86.7 us
    reduce_scatter x1, waiting for transfers between devices, on_device(): lax.psum_scatter(jnp.dot(all_piece, rows, preferred_element_type=jnp.floa...  66.7 us
    reduce_scatter x1, waiting for transfers between devices, on_device(): lax.psum_scatter(outage_rows, 'line', scatter_dimension=0, tiled=True)  59.7 us
    unnamed x5, waiting for transfers between devices  59.6 us
    dot_general x16, other arithmetic, contingency(): jnp.einsum('smk,mk->sk', raw_slope, lodf, precision=lax.Precision.HIGHEST)  56 us
    reduce_sum x16, other arithmetic, contingency(): direct = jnp.sum(raw_slope, axis=2) / outage_total  53.4 us
    all_gather x1, blocking collectives, on_device(): all_piece = lax.all_gather(piece, 'bus', axis=0, tiled=True)  47.8 us
    all_gather x1, blocking collectives, on_device(): sens_total = lax.all_gather(sens_mine, 'line', axis=1, tiled=True)  16.9 us
  transfers between devices with their start and end apart: 5, of which 5 were waited for; matrix products, arithmetic and copies ran while one was open for 2% of the time, Pallas kernels for 0%

profile of v1, /device:TPU:16, one launch (start us, length us, event | category | flops | bytes accessed | tf_op | source)
XLA Modules:
  0.0 514.4 jit_solution(11879025675101448193)
XLA Ops:
  15.3 4.9 subtract_convert_fusion
  20.3 59.7 %reduce-scatter.7.cloned.1.call-done = bf16[32,1024]{1,0:T(8,128)(2,1)} async-done(((bf16[512,1024]{1,0:T(8,128)(2,1)}), bf16[32,1024]{1,0:T(8,128)(2,1)}) %reduce-scatter.7.cloned.1.call-update) | async-done | bytes 65552 | tf_op jit(solution)/shard_map/reduce_scatter | solution.py:52
  80.0 4.2 fusion.5
  84.2 86.7 %reduce-scatter.9.cloned.1.call-done = f32[64,416]{1,0:T(8,128)} async-done(((f32[1024,416]{1,0:T(8,128)}), f32[64,416]{1,0:T(8,128)}) %reduce-scatter.9.cloned.1.call-update) | async-done | bytes 106512 | tf_op jit(solution)/shard_map/reduce_scatter | solution.py:58
  172.6 4.5 all-to-all-start
  178.4 5.3 %all-to-all-done = f32[16,1,2048]{2,1,0:T(1,128)S(1)} async-done(((f32[16,1,2048]{2,1,0:T(1,128)}), f32[16,1,2048]{2,1,0:T(1,128)S(1)}, u32[]{:S(2)}, u32[]{:S(2)}) %all-to-all-start) | async-done | bytes 131104 | tf_op jit(solution)/shard_map/all_to_all | solution.py:13
  185.9 119.4 %while.12 = (s32[]{:T(128)}, f32[16,4,384]{2,1,0:T(4,128)}, f32[16,4,512]{2,1,0:T(4,128)S(1)}, f32[16,4,384]{2,1,0:T(4,128)S(1)}, f32[384,512]{1,0:T(8,128)}, /*...) while((s32[]{:T(128)}, f32[16,4,384]{2,1,0:T(4,128)}, f32[16,4,512]{2,1,0:T(4,128)S(1)}, ...), condition=%wide.region_4.5_spmd, body=%wide.region_2.4_spmd.sunk | while | flops 24377344 | bytes 2462829 | solution.py:64
  189.3 3.5 multiply_reduce_fusion.2
  196.8 3.5 multiply_reduce_fusion.2
  204.2 3.5 multiply_reduce_fusion.2
  211.7 3.5 multiply_reduce_fusion.2
  226.6 3.5 multiply_reduce_fusion.2
  241.5 3.5 multiply_reduce_fusion.2
  249.0 3.5 multiply_reduce_fusion.2
  263.9 3.5 multiply_reduce_fusion.2
  278.8 3.5 multiply_reduce_fusion.2
  286.3 3.5 multiply_reduce_fusion.2
  293.7 3.5 multiply_reduce_fusion.2
  301.2 3.5 multiply_reduce_fusion.2
  307.3 59.5 %reduce-scatter.13.cloned.1.call-done = f32[32,72]{1,0:T(8,128)} async-done(((f32[512,72]{1,0:T(8,128)}), f32[32,72]{1,0:T(8,128)}) %reduce-scatter.13.cloned.1.call-update) | async-done | bytes 9232
  368.4 16.9 %all_gather.6 = f32[64,512]{0,1:T(8,128)S(1)} all-gather(f32[64,32]{0,1:T(8,128)} %bitcast.45), channel_id=1, replica_groups=mesh['bus'=16,'line'=16] {'line'}, dimensions={1}, use_global_device_ids=true | all-gather | bytes 139264 | tf_op jit(solution)/shard_map/all_gather | solution.py:77
  386.0 47.8 %all_gather.7 = bf16[1024,416]{1,0:T(8,128)(2,1)S(1)} all-gather(bf16[64,416]{1,0:T(8,128)(2,1)S(1)} %pad_maximum_fusion.3), channel_id=1, replica_groups=mesh['bus'=16,'line'=16] {'bus'}, dimensions={0}, use_global_device_ids=true | all-gather | bytes 905216 | tf_op jit(solution)/shard_map/all_gather | solution.py:87
  433.8 4.0 fusion.4
  439.4 66.7 %reduce-scatter.11.cloned.1.call-done = f32[64,1024]{1,0:T(8,128)} async-done(((f32[1024,1024]{1,0:T(8,128)}), f32[64,1024]{1,0:T(8,128)}) %reduce-scatter.11.cloned.1.call-update) | async-done | bytes 262160 | tf_op jit(solution)/shard_map/reduce_scatter | solution.py:89
  (149 shorter events, 97.8 us)
Async XLA Ops:
  7.2 1.6 copy-start
  7.2 72.8 %reduce-scatter.7.cloned.1.call-start = ((), (), s32[]{:S(2)}) async-start(), calls=%async_computation.5 | async-start | bytes 1114112 | tf_op jit(solution)/shard_map/reduce_scatter | solution.py:52
  10.8 1.3 copy-start.4
  12.1 158.8 %reduce-scatter.9.cloned.1.call-start = ((), (), s32[]{:S(2)}) async-start(), calls=%async_computation.6 | async-start | bytes 2228224 | tf_op jit(solution)/shard_map/reduce_scatter | solution.py:58
  12.2 3.1 copy-start.3
  12.2 3.1 copy-start.6
  15.3 64.7 %copy-start.1 = (bf16[384,1024]{1,0:T(8,128)(2,1)S(1)}, bf16[384,1024]{1,0:T(8,128)(2,1)}, u32[]{:S(2)}) copy-start(bf16[384,1024]{1,0:T(8,128)(2,1)} %broadcast_select_fusion) | copy-start | bytes 2359300
  84.2 93.1 %copy-start.5 = (s32[512]{0:T(512)S(1)}, s32[512]{0:T(512)}, u32[]{:S(2)}) copy-start(s32[512]{0:T(512)} %param.18) | copy-start | bytes 6148
  84.2 101.8 %copy-start.8 = (f32[384]{0:T(512)S(1)}, f32[384]{0:T(512)}, u32[]{:S(2)}) copy-start(f32[384]{0:T(512)} %param.16) | copy-start | bytes 4612
  172.6 11.2 %all-to-all-start = ((f32[16,1,2048]{2,1,0:T(1,128)}), f32[16,1,2048]{2,1,0:T(1,128)S(1)}, u32[]{:S(2)}, u32[]{:S(2)}) async-start(f32[16,1,2048]{2,1,0:T(1,128)} %reshape.80), calls=%async_computation.2 | async-start | bytes 262144 | tf_op jit(solution)/shard_map/all_to_all | solution.py:13
  177.1 189.7 %reduce-scatter.13.cloned.1.call-start = ((), (), s32[]{:S(2)}) async-start(), calls=%async_computation.8 | async-start | bytes 278528
  305.3 128.5 %copy-start.2 = (bf16[384,1024]{1,0:T(8,128)(2,1)S(1)}, bf16[384,1024]{1,0:T(8,128)(2,1)}, u32[]{:S(2)}) copy-start(bf16[384,1024]{1,0:T(8,128)(2,1)} %broadcast_select_fusion) | copy-start | bytes 2359300
  306.3 199.9 %reduce-scatter.11.cloned.1.call-start = ((), (), s32[]{:S(2)}) async-start(), calls=%async_computation.7 | async-start | bytes 4456448 | tf_op jit(solution)/shard_map/reduce_scatter | solution.py:89
  437.8 68.3 %copy-start.7 = (f32[1024]{0:T(1024)S(1)}, f32[1024]{0:T(1024)}, u32[]{:S(2)}) copy-start(f32[1024]{0:T(1024)} %param.19) | copy-start | bytes 12292
Sparse Core Ops, SparseCore 0:
  12.2 67.7 reduce-scatter.6
  84.3 86.5 reduce-scatter.8
  306.4 60.3 reduce-scatter.12
  438.0 68.1 reduce-scatter.10
